TPU v7x, 32 devices: a whole 2x2x4 slice. The times are simulated.
32 devices in a mesh: region: 4 (over y, x), col: 8 (over z, core).
Axes of the slice: x: 2, y: 2, z: 4, core: 2. Of those that a mesh axis runs over, the one named last changes fastest.
Arguments:
- tiles: float32 [1536, 128, 128], P(('region', 'col')), may hold values from -0.109375 to 0.109375
- tile_rows: int32 [1536], P(('region', 'col')), may hold values from 0 to 1
- tile_cols: int32 [1536], P(('region', 'col')), may hold values from 0 to 15
- tile_count: int32 [32], P(('region', 'col')), may hold values from 12 to 48, as said below
- rhs: float32 [64, 128], P(('region', 'col')), may hold values from -6 to 6
- base_cost: float32 [64, 128], P(('region', 'col')), may hold values from 0.1 to 1
- upper: float32 [64, 128], P(('region', 'col')), may hold values from 0.5 to 4
- primal: float32 [64, 16, 128], P(('region', 'col')), may hold values from 0 to 1
- dual: float32 [64, 16, 128], P(('region', 'col')), may hold values from 0 to 1
- price_levels: float32 [32, 128], replicated, may hold values from 0.5 to 2
- scenario_ids: int32 [16], replicated, may hold values from 0 to 31
Outputs:
- primal_out: float32 [64, 16, 128], P(('region', 'col'))
- dual_out: float32 [64, 16, 128], P(('region', 'col'))
- weight_out: float32 [16], replicated
Inputs may be any that keep to these rules, and one draw needn't show every extreme that they name: `tile_count`: slots at or past a device's count are padding and hold no part of the matrix; in every draw some device has all 48 slots live.
All inputs are finite; a program needn't handle non-finite values.
Results may differ from a plain program's by a relative error of at most 0.0001.
Values sent between devices are 32-bit elements; how exact they have to be, the bound alone decides.
No kernel may reach another device: no remote copies, remote signals or barrier semaphores. Data moves between devices by JAX's collectives and lax.ppermute only.
A program may use at most 64 MiB of HBM per device.

v0:
```python
import jax
import jax.numpy as jnp
from jax import lax
from jax.sharding import PartitionSpec as P

ITERS = 2


def local(
    tiles,
    tile_rows,
    tile_cols,
    tile_count,
    rhs,
    base_cost,
    upper,
    primal,
    dual,
    price_levels,
    scenario_ids,
):
    hp = lax.Precision.HIGHEST
    ntiles = tiles.shape[0]
    row_blocks = rhs.shape[0]
    own_blocks = base_cost.shape[0]
    scenarios = primal.shape[1]
    lanes = primal.shape[2]
    region_blocks = own_blocks * lax.axis_size("col")
    devices = lax.axis_size(("region", "col"))
    live = (jnp.arange(ntiles, dtype=jnp.int32) < tile_count[0]).astype(jnp.float32)
    row_select = (tile_rows[:, None] == jnp.arange(row_blocks, dtype=jnp.int32)[None, :]).astype(
        jnp.float32
    )
    row_live = row_select * live[:, None]
    col_select = (tile_cols[:, None] == jnp.arange(region_blocks, dtype=jnp.int32)[None, :]).astype(
        jnp.float32
    )
    col_live = col_select * live[:, None]
    choose = (
        scenario_ids[:, None] == jnp.arange(price_levels.shape[0], dtype=jnp.int32)[None, :]
    ).astype(jnp.float32)
    factor = jnp.dot(choose, price_levels, precision=hp)
    cost = base_cost[:, None, :] * factor[None, :, :]
    local_a = jnp.sum(jnp.sum(tiles * tiles, axis=(1, 2)) * live)
    local_c = jnp.sum(cost * cost, axis=(0, 2))
    local_b = jnp.sum(rhs * rhs)
    sq_a, sq_c, sq_b = lax.psum((local_a, local_c, local_b), ("region", "col"))
    eta = 0.5 / jnp.sqrt(sq_a / (lanes * row_blocks * devices))
    weight = jnp.sqrt(sq_c) / jnp.sqrt(sq_b)
    width = scenarios * lanes
    for step in range(ITERS):
        tau = (eta / weight)[None, :, None]
        sigma = (eta * weight)[None, :, None]
        dual_rows = jnp.dot(row_select, dual.reshape(row_blocks, width), precision=hp).reshape(
            ntiles, scenarios, lanes
        )
        contrib = jnp.einsum("tij,tsi->tsj", tiles, dual_rows, precision=hp)
        flat_terms = contrib.reshape(ntiles, width)
        partial_value = jnp.dot(col_live.T, flat_terms, precision=hp).reshape(
            region_blocks, scenarios, lanes
        )
        grad = lax.psum_scatter(partial_value, "col", scatter_dimension=0, tiled=True)
        new_primal = jnp.clip(primal - tau * (cost - grad), 0.0, upper[:, None, :])
        point = 2.0 * new_primal - primal
        region_point = lax.all_gather(point, "col", axis=0, tiled=True)
        selected = jnp.dot(
            col_select, region_point.reshape(region_blocks, width), precision=hp
        ).reshape(ntiles, scenarios, lanes)
        image = jnp.einsum("tij,tsj->tsi", tiles, selected, precision=hp)
        product = jnp.dot(row_live.T, image.reshape(ntiles, width), precision=hp).reshape(
            row_blocks, scenarios, lanes
        )
        new_dual = jnp.maximum(dual + sigma * (rhs[:, None, :] - product), 0.0)
        local_x = jnp.sum((new_primal - primal) ** 2, axis=(0, 2))
        local_y = jnp.sum((new_dual - dual) ** 2, axis=(0, 2))
        step_x = lax.psum(local_x, ("region", "col"))
        step_y = lax.psum(local_y, ("region", "col"))
        weight = jnp.sqrt(weight * jnp.sqrt((step_x + 1e-06) / (step_y + 1e-06)))
        primal, dual = (new_primal, new_dual)
    return (primal, dual, weight)


def solution(mesh):
    placed = (
        P(("region", "col"), None, None),
        P(("region", "col")),
        P(("region", "col")),
        P(("region", "col")),
        P(("region", "col"), None),
        P(("region", "col"), None),
        P(("region", "col"), None),
        P(("region", "col"), None, None),
        P(("region", "col"), None, None),
        P(),
        P(),
    )
    return jax.shard_map(
        local,
        mesh=mesh,
        in_specs=placed,
        out_specs=(P(("region", "col"), None, None), P(("region", "col"), None, None), P()),
        check_vma=False,
    )
```

profile of v0, /device:TPU:10, one launch (start us, length us, event | category | flops | bytes accessed | tf_op | source)
XLA Modules:
  0.0 194.1 jit_solution(15329960555821616585)
XLA Ops:
  8.1 1.2 fusion.37
  9.3 4.7 %fusion.18 = f32[48,16,128]{2,1,0:T(8,128)S(1)} fusion(f32[48,128,128]{2,1,0:T(8,128)} %param.11, f32[48,16,128]{2,0,1:T(8,128)S(1)} %fusion.37), kind=kOutput, calls=%fused_computation.23 | convolution fusion | flops 150994944 | bytes 3932160 | tf_op jit(solution)/shard_map/tij,tsi->tsj/dot_general | solution.py:57
  14.1 0.4 fusion.9
  14.5 0.7 copy.80
  15.3 0.5 multiply_reduce_fusion
  15.7 0.6 fusion.68
  16.6 0.6 multiply_reduce_fusion.5
  17.2 41.5 %all-reduce.2 = (f32[16]{0:T(128)S(1)}, f32[]{:T(128)}, f32[]{:T(128)}) all-reduce(f32[16]{0:T(128)S(1)} %fusion.26, f32[]{:T(128)} %fusion.68, f32[]{:T(128)} %multiply_reduce_fusion.5), channel_id=1, replica_groups=mesh['region'=4,'col'=8] {'region','col'}, use_global_device_ids=true, to_apply=%region_6.0 | all-reduce | flops 18 | bytes 144 | tf_op jit(solution)/shard_map/psum | solution.py:47
  60.2 0.9 multiply_reduce_fusion.4
  61.1 13.1 %all_gather.6 = f32[16,16,128]{2,1,0:T(8,128)S(1)} all-gather(f32[2,16,128]{2,1,0:T(8,128)S(1)} %multiply_subtract_fusion.3), channel_id=1, replica_groups=mesh['region'=4,'col'=8] {'col'}, dimensions={0}, use_global_device_ids=true | all-gather | bytes 147456 | tf_op jit(solution)/shard_map/all_gather | solution.py:65
  74.6 5.0 %fusion.16 = f32[48,16,128]{2,1,0:T(8,128)S(1)} fusion(f32[48,128,128]{2,1,0:T(8,128)S(1)} %copy-done.1, f32[48,16,128]{2,0,1:T(8,128)S(1)} %fusion.23), kind=kOutput, calls=%fused_computation.21 | convolution fusion | flops 150994944 | bytes 3932160 | tf_op jit(solution)/shard_map/tij,tsj->tsi/dot_general | solution.py:69
  79.5 0.4 fusion.6
  80.2 0.4 fusion.35
  80.6 2.9 %fusion.14 = f32[48,16,128]{2,1,0:T(8,128)S(1)} fusion(f32[48,128,128]{2,1,0:T(8,128)S(1)} %copy-done.1, f32[48,16,128]{2,0,1:T(8,128)S(1)} %fusion.35), kind=kOutput, calls=%fused_computation.19 | convolution fusion | flops 150994944 | bytes 3932160 | tf_op jit(solution)/shard_map/tij,tsi->tsj/dot_general | solution.py:57
  83.4 0.4 fusion.3
  83.9 0.7 copy.87
  84.6 40.5 %all-reduce.1 = (f32[16]{0:T(128)S(1)}, f32[16]{0:T(128)S(1)}) all-reduce(f32[16]{0:T(128)S(1)} %get-tuple-element.30, f32[16]{0:T(128)S(1)} %get-tuple-element.28), channel_id=1, replica_groups=mesh['region'=4,'col'=8] {'region','col'}, use_global_device_ids=true, to_apply=%region_11.12 | all-reduce | flops 32 | bytes 256 | tf_op jit(solution)/shard_map/psum | solution.py:77
  125.1 0.9 multiply_reduce_fusion.2
  126.0 12.4 %all_gather.7 = f32[16,16,128]{2,1,0:T(8,128)S(1)} all-gather(f32[2,16,128]{2,1,0:T(8,128)S(1)} %multiply_subtract_fusion.2), channel_id=1, replica_groups=mesh['region'=4,'col'=8] {'col'}, dimensions={0}, use_global_device_ids=true | all-gather | bytes 147456 | tf_op jit(solution)/shard_map/all_gather | solution.py:65
  138.8 5.0 %fusion.12 = f32[48,16,128]{2,1,0:T(8,128)S(1)} fusion(f32[48,128,128]{2,1,0:T(8,128)S(1)} %copy-done.1, f32[48,16,128]{2,0,1:T(8,128)S(1)} %fusion.20), kind=kOutput, calls=%fused_computation.17 | convolution fusion | flops 150994944 | bytes 3932160 | tf_op jit(solution)/shard_map/tij,tsj->tsi/dot_general | solution.py:69
  143.8 0.4 fusion
  144.2 0.8 multiply_reduce_fusion.1
  145.0 41.7 %all-reduce = (f32[16]{0:T(128)S(1)}, f32[16]{0:T(128)S(1)}) all-reduce(f32[16]{0:T(128)S(1)} %get-tuple-element.24, f32[16]{0:T(128)S(1)} %get-tuple-element.22), channel_id=1, replica_groups=mesh['region'=4,'col'=8] {'region','col'}, use_global_device_ids=true, to_apply=%region_16.17 | all-reduce | flops 32 | bytes 256 | tf_op jit(solution)/shard_map/psum | solution.py:77
  186.7 0.5 multiply_sqrt_fusion
  (39 shorter events, 1.5 us)
Async XLA Ops:
  7.2 9.2 %copy-start = (f32[32,128]{1,0:T(8,128)S(1)}, f32[32,128]{1,0:T(8,128)}, u32[]{:S(2)}) copy-start(f32[32,128]{1,0:T(8,128)} %param.20) | copy-start | bytes 49156
  7.2 8.1 %copy-start.1 = (f32[48,128,128]{2,1,0:T(8,128)S(1)}, f32[48,128,128]{2,1,0:T(8,128)}, u32[]{:S(2)}) copy-start(f32[48,128,128]{2,1,0:T(8,128)} %param.11) | copy-start | bytes 9437188
  7.2 6.9 %copy-start.7 = (s32[48]{0:T(128)S(1)}, s32[48]{0:T(128)}, u32[]{:S(2)}) copy-start(s32[48]{0:T(128)} %param.13) | copy-start | bytes 580
  7.2 53.0 %reduce-scatter.3.cloned.1.call-start = ((), (), s32[]{:S(2)}) async-start(), calls=%async_computation.2 | async-start | bytes 147456 | tf_op jit(solution)/shard_map/reduce_scatter | solution.py:62
  9.3 7.0 %copy-start.10 = (s32[16]{0:T(128)S(1)}, s32[16]{0:T(128)}, u32[]{:S(2)}) copy-start(s32[16]{0:T(128)} %param.21) | copy-start | bytes 196
  9.3 7.2 %copy-start.5 = (f32[2,128]{1,0:T(2,128)S(1)}, f32[2,128]{1,0:T(2,128)}, u32[]{:S(2)}) copy-start(f32[2,128]{1,0:T(2,128)} %param.16) | copy-start | bytes 3076
  9.3 7.3 %copy-start.9 = (f32[2,128]{1,0:T(2,128)S(1)}, f32[2,128]{1,0:T(2,128)}, u32[]{:S(2)}) copy-start(f32[2,128]{1,0:T(2,128)} %param.15) | copy-start | bytes 3076
  9.3 50.9 %copy-start.3 = (f32[2,16,128]{2,1,0:T(8,128)S(1)}, f32[2,16,128]{2,1,0:T(8,128)}, u32[]{:S(2)}) copy-start(f32[2,16,128]{2,1,0:T(8,128)} %param.18) | copy-start | bytes 49156
  9.3 50.9 %copy-start.8 = (f32[2,128]{1,0:T(2,128)S(1)}, f32[2,128]{1,0:T(2,128)}, u32[]{:S(2)}) copy-start(f32[2,128]{1,0:T(2,128)} %param.17) | copy-start | bytes 3076
  15.2 109.9 %reduce-scatter.5.cloned.1.call-start = ((), (), s32[]{:S(2)}) async-start(), calls=%async_computation.3 | async-start | bytes 147456 | tf_op jit(solution)/shard_map/reduce_scatter | solution.py:62
  15.7 63.8 %copy-start.6 = (s32[48]{0:T(128)S(1)}, s32[48]{0:T(128)}, u32[]{:S(2)}) copy-start(s32[48]{0:T(128)} %param.12) | copy-start | bytes 580
  15.7 64.3 %copy-start.2 = (f32[2,16,128]{2,1,0:T(8,128)S(1)}, f32[2,16,128]{2,1,0:T(8,128)}, u32[]{:S(2)}) copy-start(f32[2,16,128]{2,1,0:T(8,128)} %param.19) | copy-start | bytes 49156
  126.0 61.2 %copy-start.4 = (f32[2,16,128]{2,1,0:T(8,128)}, f32[2,16,128]{2,1,0:T(8,128)S(1)}, u32[]{:S(2)}) copy-start(f32[2,16,128]{2,1,0:T(8,128)S(1)} %get-tuple-element.23) | copy-start | bytes 49156
Sparse Core Ops, SparseCore 0:
  15.3 27.7 reduce-scatter.2
  84.7 26.8 reduce-scatter.4
where the time goes:
time: 195 us; the launch traced here: 194 us
  blocking collectives  149 us (76%)
  matrix products  21.7 us (11%)
  between operations  16.4 us (8%)
  other arithmetic  5.15 us (3%)
    psum x2, blocking collectives, local(): step_y = lax.psum(local_y, ('region', 'col'))  82.2 us
    psum x1, blocking collectives, local(): sq_a, sq_c, sq_b = lax.psum((local_a, local_c, local_b), ('region', 'col'))  41.5 us
    all_gather x2, blocking collectives, local(): region_point = lax.all_gather(point, 'col', axis=0, tiled=True)  25.5 us
    dot_general x2, matrix products, local(): image = jnp.einsum('tij,tsj->tsi', tiles, selected, precision=hp)  9.98 us
    dot_general x2, matrix products, local(): contrib = jnp.einsum('tij,tsi->tsj', tiles, dual_rows, precision=hp)  7.59 us
  transfers between devices with their start and end apart: 2, of which 0 were waited for; matrix products, arithmetic and copies ran while one was open for 1% of the time, Pallas kernels for 0%

commit v1 on v0

--- a/solution.py
+++ b/solution.py
@@ -74,7 +74,7 @@
         local_x = jnp.sum((new_primal - primal) ** 2, axis=(0, 2))
         local_y = jnp.sum((new_dual - dual) ** 2, axis=(0, 2))
         step_x = lax.psum(local_x, ("region", "col"))
-        step_y = lax.psum(local_y, ("region", "col"))
+        step_y = lax.psum(lax.psum(local_y, "col"), "region")
         weight = jnp.sqrt(weight * jnp.sqrt((step_x + 1e-06) / (step_y + 1e-06)))
         primal, dual = (new_primal, new_dual)
     return (primal, dual, weight)

time: 195 us -> 271 us (1.39)
  blocking collectives: 149 us -> 198 us
  waiting for transfers between devices: 0.07 us -> 25.9 us
    psum x2 -> x6, blocking collectives: 82.2 us -> 129 us  [the longest x2 86.2 us: local(): step_x = lax.psum(local_x, ('region', 'col'))]
    reduce_scatter x2, waiting for transfers between devices: 0.04 us -> 25.9 us  [local(): lax.psum_scatter(partial_value, 'col', scatter_dimension=0, tiled=True)]
  transfers between devices with their start and end apart: 2 -> 2, of which waited for: 0 -> 1; matrix products, arithmetic and copies ran while one was open for 1% -> 1% of each run, Pallas kernels for 0% -> 0%
where the time goes in v1:
time: 271 us; the launch traced here: 269 us
  blocking collectives  198 us (73%)
  waiting for transfers between devices  25.9 us (10%)
  matrix products  21.7 us (8%)
  between operations  16.4 us (6%)
  other arithmetic  5.15 us (2%)
    psum x2, blocking collectives, local(): step_x = lax.psum(local_x, ('region', 'col'))  86.2 us
    psum x4, blocking collectives, local(): step_y = lax.psum(lax.psum(local_y, 'col'), 'region')  43.2 us
    psum x1, blocking collectives, local(): sq_a, sq_c, sq_b = lax.psum((local_a, local_c, local_b), ('region', 'col'))  41.5 us
    all_gather x2, blocking collectives, local(): region_point = lax.all_gather(point, 'col', axis=0, tiled=True)  27.2 us
    reduce_scatter x2, waiting for transfers between devices, local(): lax.psum_scatter(partial_value, 'col', scatter_dimension=0, tiled=True)  25.9 us
    dot_general x2, matrix products, local(): image = jnp.einsum('tij,tsj->tsi', tiles, selected, precision=hp)  9.98 us
    dot_general x2, matrix products, local(): contrib = jnp.einsum('tij,tsi->tsj', tiles, dual_rows, precision=hp)  7.59 us
  transfers between devices with their start and end apart: 2, of which 1 were waited for; matrix products, arithmetic and copies ran while one was open for 1% of the time, Pallas kernels for 0%

profile of v1, /device:TPU:10, one launch (start us, length us, event | category | flops | bytes accessed | tf_op | source)
XLA Modules:
  0.0 268.8 jit_solution(5853221392312416262)
XLA Ops:
  8.1 1.2 fusion.37
  9.3 4.7 %fusion.18 = f32[48,16,128]{2,1,0:T(8,128)S(1)} fusion(f32[48,128,128]{2,1,0:T(8,128)} %param.11, f32[48,16,128]{2,0,1:T(8,128)S(1)} %fusion.37), kind=kOutput, calls=%fused_computation.23 | convolution fusion | flops 150994944 | bytes 3932160 | tf_op jit(solution)/shard_map/tij,tsi->tsj/dot_general | solution.py:57
  14.5 0.7 copy.80
  15.3 0.5 multiply_reduce_fusion
  15.7 0.6 fusion.68
  16.6 0.6 multiply_reduce_fusion.5
  17.2 41.5 %all-reduce = (f32[16]{0:T(128)S(1)}, f32[]{:T(128)}, f32[]{:T(128)}) all-reduce(f32[16]{0:T(128)S(1)} %fusion.26, f32[]{:T(128)} %fusion.68, f32[]{:T(128)} %multiply_reduce_fusion.5), channel_id=1, replica_groups=mesh['region'=4,'col'=8] {'region','col'}, use_global_device_ids=true, to_apply=%region_6.0 | all-reduce | flops 18 | bytes 144 | tf_op jit(solution)/shard_map/psum | solution.py:47
  60.2 0.9 multiply_reduce_fusion.4
  61.1 12.9 %all_gather.6 = f32[16,16,128]{2,1,0:T(8,128)S(1)} all-gather(f32[2,16,128]{2,1,0:T(8,128)S(1)} %multiply_subtract_fusion.3), channel_id=1, replica_groups=mesh['region'=4,'col'=8] {'col'}, dimensions={0}, use_global_device_ids=true | all-gather | bytes 147456 | tf_op jit(solution)/shard_map/all_gather | solution.py:65
  74.4 5.0 %fusion.16 = f32[48,16,128]{2,1,0:T(8,128)S(1)} fusion(f32[48,128,128]{2,1,0:T(8,128)S(1)} %copy-done.1, f32[48,16,128]{2,0,1:T(8,128)S(1)} %fusion.23), kind=kOutput, calls=%fused_computation.21 | convolution fusion | flops 150994944 | bytes 3932160 | tf_op jit(solution)/shard_map/tij,tsj->tsi/dot_general | solution.py:69
  80.0 13.3 %psum.67 = f32[16]{0:T(128)S(1)} all-reduce(f32[16]{0:T(128)S(1)} %get-tuple-element.26), channel_id=1, replica_groups=mesh['region'=4,'col'=8] {'col'}, use_global_device_ids=true, to_apply=%region_11.12 | all-reduce | flops 16 | bytes 128 | tf_op jit(solution)/shard_map/psum | solution.py:77
  93.3 42.8 %psum.66 = f32[16]{0:T(128)S(1)} all-reduce(f32[16]{0:T(128)S(1)} %get-tuple-element.24), channel_id=1, replica_groups=mesh['region'=4,'col'=8] {'region','col'}, use_global_device_ids=true, to_apply=%region_9.10 | all-reduce | flops 16 | bytes 128 | tf_op jit(solution)/shard_map/psum | solution.py:76
  136.1 8.2 %psum.68 = f32[16]{0:T(128)S(1)} all-reduce(f32[16]{0:T(128)S(1)} %psum.67), channel_id=1, replica_groups=mesh['region'=4,'col'=8] {'region'}, use_global_device_ids=true, to_apply=%region_12.13 | all-reduce | flops 16 | bytes 128 | tf_op jit(solution)/shard_map/psum | solution.py:77
  144.7 2.9 %fusion.14 = f32[48,16,128]{2,1,0:T(8,128)S(1)} fusion(f32[48,128,128]{2,1,0:T(8,128)S(1)} %copy-done.1, f32[48,16,128]{2,0,1:T(8,128)S(1)} %fusion.35), kind=kOutput, calls=%fused_computation.19 | convolution fusion | flops 150994944 | bytes 3932160 | tf_op jit(solution)/shard_map/tij,tsi->tsj/dot_general | solution.py:57
  148.0 0.7 copy.87
  148.7 25.8 %reduce-scatter.5.cloned.1.call-done = f32[2,16,128]{2,1,0:T(8,128)} async-done(((f32[16,16,128]{2,1,0:T(8,128)}), f32[2,16,128]{2,1,0:T(8,128)}) %reduce-scatter.5.cloned.1.call-update) | async-done | bytes 16400 | tf_op jit(solution)/shard_map/reduce_scatter | solution.py:62
  174.6 0.9 multiply_reduce_fusion.2
  175.5 14.3 %all_gather.7 = f32[16,16,128]{2,1,0:T(8,128)S(1)} all-gather(f32[2,16,128]{2,1,0:T(8,128)S(1)} %multiply_subtract_fusion.2), channel_id=1, replica_groups=mesh['region'=4,'col'=8] {'col'}, dimensions={0}, use_global_device_ids=true | all-gather | bytes 147456 | tf_op jit(solution)/shard_map/all_gather | solution.py:65
  190.1 5.0 %fusion.12 = f32[48,16,128]{2,1,0:T(8,128)S(1)} fusion(f32[48,128,128]{2,1,0:T(8,128)S(1)} %copy-done.1, f32[48,16,128]{2,0,1:T(8,128)S(1)} %fusion.20), kind=kOutput, calls=%fused_computation.17 | convolution fusion | flops 150994944 | bytes 3932160 | tf_op jit(solution)/shard_map/tij,tsj->tsi/dot_general | solution.py:69
  195.6 0.8 multiply_reduce_fusion.1
  196.4 13.7 %psum.70 = f32[16]{0:T(128)S(1)} all-reduce(f32[16]{0:T(128)S(1)} %get-tuple-element.20), channel_id=1, replica_groups=mesh['region'=4,'col'=8] {'col'}, use_global_device_ids=true, to_apply=%region_17.18 | all-reduce | flops 16 | bytes 128 | tf_op jit(solution)/shard_map/psum | solution.py:77
  210.1 43.4 %psum.69 = f32[16]{0:T(128)S(1)} all-reduce(f32[16]{0:T(128)S(1)} %get-tuple-element.18), channel_id=1, replica_groups=mesh['region'=4,'col'=8] {'region','col'}, use_global_device_ids=true, to_apply=%region_15.16 | all-reduce | flops 16 | bytes 128 | tf_op jit(solution)/shard_map/psum | solution.py:76
  253.4 8.0 %psum.71 = f32[16]{0:T(128)S(1)} all-reduce(f32[16]{0:T(128)S(1)} %psum.70), channel_id=1, replica_groups=mesh['region'=4,'col'=8] {'region'}, use_global_device_ids=true, to_apply=%region_18.19 | all-reduce | flops 16 | bytes 128 | tf_op jit(solution)/shard_map/psum | solution.py:77
  261.4 0.5 multiply_sqrt_fusion
  (43 shorter events, 3.5 us)
Async XLA Ops:
  7.2 9.2 %copy-start = (f32[32,128]{1,0:T(8,128)S(1)}, f32[32,128]{1,0:T(8,128)}, u32[]{:S(2)}) copy-start(f32[32,128]{1,0:T(8,128)} %param.20) | copy-start | bytes 49156
  7.2 8.1 %copy-start.1 = (f32[48,128,128]{2,1,0:T(8,128)S(1)}, f32[48,128,128]{2,1,0:T(8,128)}, u32[]{:S(2)}) copy-start(f32[48,128,128]{2,1,0:T(8,128)} %param.11) | copy-start | bytes 9437188
  7.2 6.9 %copy-start.7 = (s32[48]{0:T(128)S(1)}, s32[48]{0:T(128)}, u32[]{:S(2)}) copy-start(s32[48]{0:T(128)} %param.13) | copy-start | bytes 580
  7.2 53.0 %reduce-scatter.3.cloned.1.call-start = ((), (), s32[]{:S(2)}) async-start(), calls=%async_computation.2 | async-start | bytes 147456 | tf_op jit(solution)/shard_map/reduce_scatter | solution.py:62
  9.3 7.0 %copy-start.10 = (s32[16]{0:T(128)S(1)}, s32[16]{0:T(128)}, u32[]{:S(2)}) copy-start(s32[16]{0:T(128)} %param.21) | copy-start | bytes 196
  9.3 7.2 %copy-start.5 = (f32[2,128]{1,0:T(2,128)S(1)}, f32[2,128]{1,0:T(2,128)}, u32[]{:S(2)}) copy-start(f32[2,128]{1,0:T(2,128)} %param.16) | copy-start | bytes 3076
  9.3 7.3 %copy-start.9 = (f32[2,128]{1,0:T(2,128)S(1)}, f32[2,128]{1,0:T(2,128)}, u32[]{:S(2)}) copy-start(f32[2,128]{1,0:T(2,128)} %param.15) | copy-start | bytes 3076
  9.3 50.9 %copy-start.3 = (f32[2,16,128]{2,1,0:T(8,128)S(1)}, f32[2,16,128]{2,1,0:T(8,128)}, u32[]{:S(2)}) copy-start(f32[2,16,128]{2,1,0:T(8,128)} %param.18) | copy-start | bytes 49156
  9.3 50.9 %copy-start.8 = (f32[2,128]{1,0:T(2,128)S(1)}, f32[2,128]{1,0:T(2,128)}, u32[]{:S(2)}) copy-start(f32[2,128]{1,0:T(2,128)} %param.17) | copy-start | bytes 3076
  15.2 159.4 %reduce-scatter.5.cloned.1.call-start = ((), (), s32[]{:S(2)}) async-start(), calls=%async_computation.3 | async-start | bytes 147456 | tf_op jit(solution)/shard_map/reduce_scatter | solution.py:62
  15.7 63.7 %copy-start.6 = (s32[48]{0:T(128)S(1)}, s32[48]{0:T(128)}, u32[]{:S(2)}) copy-start(s32[48]{0:T(128)} %param.12) | copy-start | bytes 580
  15.7 64.1 %copy-start.2 = (f32[2,16,128]{2,1,0:T(8,128)S(1)}, f32[2,16,128]{2,1,0:T(8,128)}, u32[]{:S(2)}) copy-start(f32[2,16,128]{2,1,0:T(8,128)} %param.19) | copy-start | bytes 49156
  175.5 86.5 %copy-start.4 = (f32[2,16,128]{2,1,0:T(8,128)}, f32[2,16,128]{2,1,0:T(8,128)S(1)}, u32[]{:S(2)}) copy-start(f32[2,16,128]{2,1,0:T(8,128)S(1)} %get-tuple-element.19) | copy-start | bytes 49156
Sparse Core Ops, SparseCore 0:
  15.3 27.7 reduce-scatter.2
  148.8 25.7 reduce-scatter.4
